TPU v7x, 256 devices: a whole 4x4x8 slice. The times are simulated.
256 devices in a mesh: seq: 16 (over y_lo, z), tm: 8 (over x, core), dp: 2 (over y_hi).
Axes of the slice: x: 4, y: 4 (y_hi: 2, y_lo: 2; y = y_hi * 2 + y_lo), z: 8, core: 2. Of those that a mesh axis runs over, the one named last changes fastest.
Arguments:
- queries: bfloat16 [16384, 8, 128], P(('dp', 'seq'), 'tm'), parts along dimension 0, may hold values from -6 to 6
- keys: bfloat16 [16384, 8, 128], P(('dp', 'seq'), 'tm'), parts along dimension 0, may hold values from -6 to 6
- values: bfloat16 [16384, 8, 128], P(('dp', 'seq'), 'tm'), parts along dimension 0, may hold values from -6 to 6
- token_cell: int32 [512], P('seq'), may hold values from 0 to 511, each once
- head_weight: bfloat16 [8, 128, 384], P('tm'), may hold values from -2 to 2
- norm_gain: float32 [384], replicated, may hold values from 0.1 to 1.9
- time_weight: bfloat16 [3, 384, 768], replicated, may hold values from -0.1875 to 0.1875
- frame_clip: int32 [32], P('dp'), parts along dimension 0, may hold values from 0 to 2, never falling along the last dimension, each value on 1 to 8 neighbouring positions
- cotangent: bfloat16 [32, 512, 768], P(('dp', 'tm'), 'seq'), parts along dimension 0, may hold values from -6 to 6
Outputs:
- grad_queries: bfloat16 [16384, 8, 128], P(('dp', 'seq'), 'tm'), parts along dimension 0
- grad_keys: bfloat16 [16384, 8, 128], P(('dp', 'seq'), 'tm'), parts along dimension 0
- grad_values: bfloat16 [16384, 8, 128], P(('dp', 'seq'), 'tm'), parts along dimension 0
There are 2 independent parts, one for each index of `dp`. A program takes and returns all parts, laid end to end along the dimension named above; an argument that names none is the same for every part. Nothing has to cross between parts.
Inputs may be any that keep to these rules, and one draw needn't show every extreme that they name: `token_cell`: a permutation of the 512 cells. `frame_clip`: never falls along the frames.
All inputs are finite; a program needn't handle non-finite values.
Results may differ from a plain program's by a relative error of at most 0.023.
Values may be sent and summed in bfloat16 or wider, within the bound.
No kernel may reach another device: no remote copies, remote signals or barrier semaphores. Data moves between devices by JAX's collectives and lax.ppermute only.
A program may use at most 64 MiB of HBM per device.

v0:
```python
import math
import jax
import jax.numpy as jnp
from jax import lax
from jax.sharding import PartitionSpec as P

HD = 128
GRID_W = 32


def shifted(value, axis, steps):
    count = lax.axis_size(axis)
    initial, last = (max(0, -steps), min(count, count - steps))
    return lax.ppermute(value, axis, [(source, source + steps) for source in range(initial, last)])


def frequencies(pair_count):
    return 1.0 / 10000.0 ** (jnp.arange(pair_count, dtype=jnp.float32) / pair_count)


def rope_tables(frame_pos, cell_ids):
    pair_count = HD // 2
    part_side = pair_count // 3
    part_time = pair_count - 2 * part_side
    grid_row = (cell_ids // GRID_W).astype(jnp.float32)
    grid_col = (cell_ids % GRID_W).astype(jnp.float32)
    angles = jnp.concatenate(
        [
            frame_pos.astype(jnp.float32)[:, None] * frequencies(part_time)[None, :],
            grid_row[:, None] * frequencies(part_side)[None, :],
            grid_col[:, None] * frequencies(part_side)[None, :],
        ],
        axis=1,
    )
    return (jnp.cos(angles), jnp.sin(angles))


def rotate(vectors, cos_table, sin_table, direction):
    layout = vectors.shape
    paired = vectors.reshape(layout[:-1] + (layout[-1] // 2, 2))
    former = paired[..., 0]
    latter = paired[..., 1]
    out_former = former * cos_table - direction * latter * sin_table
    out_latter = direction * former * sin_table + latter * cos_table
    return jnp.stack([out_former, out_latter], axis=-1).reshape(layout)


def tap_mask(frame_clip):
    frame_total = frame_clip.shape[0]
    frame_ids = jnp.arange(frame_total, dtype=jnp.int32)
    columns = []
    for offset in range(3):
        target = frame_ids + offset
        inside = target < frame_total
        same_clip = frame_clip[jnp.minimum(target, frame_total - 1)] == frame_clip
        columns.append(jnp.logical_and(inside, same_clip).astype(jnp.float32))
    return jnp.stack(columns, axis=1)


def cross(left, right):
    return lax.dot_general(
        left, right, (((1,), (1,)), ((), ())), preferred_element_type=jnp.float32
    )


def inner(left, right):
    return lax.dot_general(
        left, right, (((0,), (0,)), ((), ())), preferred_element_type=jnp.float32
    )


def on_device(
    queries, keys, values, token_cell, head_weight, norm_gain, time_weight, frame_clip, cotangent
):
    score_scale = HD ** (-0.5)
    tok_local = queries.shape[0]
    slab_cells = token_cell.shape[0]
    span_frames = cotangent.shape[0]
    channels = head_weight.shape[2]
    frame_pos = jnp.arange(tok_local, dtype=jnp.int32) // slab_cells
    cell_ids = jnp.tile(token_cell, tok_local // slab_cells)
    cos_table, sin_table = rope_tables(frame_pos, cell_ids)
    rot_q = rotate(queries[:, 0, :].astype(jnp.float32), cos_table, sin_table, 1.0).astype(
        jnp.bfloat16
    )
    rot_k = rotate(keys[:, 0, :].astype(jnp.float32), cos_table, sin_table, 1.0).astype(
        jnp.bfloat16
    )
    plain_v = values[:, 0, :]
    keys_all, values_all = (
        lax.all_gather(rot_k, "seq", axis=0, tiled=True),
        lax.all_gather(plain_v, "seq", axis=0, tiled=True),
    )
    total_tokens = keys_all.shape[0]
    key_block = math.gcd(total_tokens, 1024)
    block_count = total_tokens // key_block

    def forward_step(block_id, state):
        running_top, running_total, running_sum = state
        key_piece = lax.dynamic_slice_in_dim(keys_all, block_id * key_block, key_block, 0)
        value_piece = lax.dynamic_slice_in_dim(values_all, block_id * key_block, key_block, 0)
        scores = cross(rot_q, key_piece) * score_scale
        new_top = jnp.maximum(running_top, jnp.max(scores, axis=1))
        factor = jnp.exp(running_top - new_top)
        weights = jnp.exp(scores - new_top[:, None])
        running_total = running_total * factor + jnp.sum(weights, axis=1)
        running_sum = running_sum * factor[:, None] + jnp.dot(
            weights.astype(jnp.bfloat16), value_piece, preferred_element_type=jnp.float32
        )
        return (new_top, running_total, running_sum)

    start_state = (
        jnp.full((tok_local,), -1e30, jnp.float32),
        jnp.zeros((tok_local,), jnp.float32),
        jnp.zeros((tok_local, HD), jnp.float32),
    )
    row_top, row_total, summed = lax.fori_loop(0, block_count, forward_step, start_state)
    attended = (summed / row_total[:, None]).astype(jnp.bfloat16)
    log_total = row_top + jnp.log(row_total)
    span_rows = span_frames * slab_cells
    mixed = (
        lax.psum_scatter(
            jnp.dot(attended, head_weight[0], preferred_element_type=jnp.float32).astype(
                jnp.bfloat16
            ),
            "tm",
            scatter_dimension=0,
            tiled=True,
        )
        .astype(jnp.float32)
        .reshape(span_frames, slab_cells, channels)
    )
    inverse = lax.rsqrt(jnp.mean(mixed * mixed, axis=2, keepdims=True) + 1e-06)
    normed = mixed * inverse * norm_gain
    mask_table = tap_mask(frame_clip)
    first_frame = lax.axis_index("tm") * span_frames
    local_mask = lax.dynamic_slice_in_dim(mask_table, first_frame, span_frames, 0)
    following = shifted(cotangent, "tm", -1)
    extended = jnp.concatenate([cotangent, following], axis=0)
    grad_act = jnp.zeros((span_frames, slab_cells, channels), jnp.float32)
    for offset in range(3):
        term = jnp.einsum(
            "fco,io->fci",
            extended[offset : offset + span_frames],
            time_weight[offset],
            preferred_element_type=jnp.float32,
        )
        grad_act = grad_act + local_mask[:, offset][:, None, None] * term
    sigmoid_n = jax.nn.sigmoid(normed)
    grad_normed = grad_act * sigmoid_n * (1.0 + normed * (1.0 - sigmoid_n))
    gained = grad_normed * norm_gain
    grad_mixed = (
        inverse * gained
        - inverse * inverse * inverse * mixed * jnp.mean(gained * mixed, axis=2, keepdims=True)
    ).astype(jnp.bfloat16)
    grad_mixed = grad_mixed.reshape(span_rows, channels)
    grad_out = cross(lax.all_gather(grad_mixed, "tm", axis=0, tiled=True), head_weight[0]).astype(
        jnp.bfloat16
    )
    row_delta = jnp.sum(grad_out.astype(jnp.float32) * attended.astype(jnp.float32), axis=1)

    def score_block(block_id):
        key_piece = lax.dynamic_slice_in_dim(keys_all, block_id * key_block, key_block, 0)
        value_piece = lax.dynamic_slice_in_dim(values_all, block_id * key_block, key_block, 0)
        scores = cross(rot_q, key_piece) * score_scale
        weights = jnp.exp(scores - log_total[:, None])
        grad_w = cross(grad_out, value_piece)
        grad_s = (weights * (grad_w - row_delta[:, None])).astype(jnp.bfloat16)
        return (key_piece, weights, grad_s)

    def query_step(block_id, grad_q):
        key_piece, weights, grad_s = score_block(block_id)
        return grad_q + jnp.dot(grad_s, key_piece, preferred_element_type=jnp.float32) * score_scale

    grad_q = lax.fori_loop(0, block_count, query_step, jnp.zeros((tok_local, HD), jnp.float32))
    fold_start = (jnp.zeros((tok_local, HD), jnp.float32), jnp.zeros((tok_local, HD), jnp.float32))
    wide_q = rot_q.astype(jnp.float32)
    wide_grad = grad_out.astype(jnp.float32)
    piece_q = lax.all_gather(wide_q, "seq", axis=0, tiled=True)
    piece_grad = lax.all_gather(wide_grad, "seq", axis=0, tiled=True)
    piece_log = lax.all_gather(log_total, "seq", axis=0, tiled=True)
    piece_delta = lax.all_gather(row_delta, "seq", axis=0, tiled=True)
    piece_count = piece_q.shape[0]
    sub_rows = math.gcd(piece_count, 1024)

    def sub_step(sub_id, inner_carry):
        grad_k, grad_v = inner_carry
        offset = sub_id * sub_rows
        query_block = lax.dynamic_slice_in_dim(piece_q, offset, sub_rows, 0).astype(jnp.bfloat16)
        grad_rows = lax.dynamic_slice_in_dim(piece_grad, offset, sub_rows, 0).astype(jnp.bfloat16)
        log_block = lax.dynamic_slice_in_dim(piece_log, offset, sub_rows, 0)
        delta_block = lax.dynamic_slice_in_dim(piece_delta, offset, sub_rows, 0)
        scores = cross(query_block, rot_k) * score_scale
        weights = jnp.exp(scores - log_block[:, None])
        grad_w = cross(grad_rows, plain_v)
        grad_s = (weights * (grad_w - delta_block[:, None])).astype(jnp.bfloat16)
        grad_k = grad_k + inner(grad_s, query_block) * score_scale
        grad_v = grad_v + inner(weights.astype(jnp.bfloat16), grad_rows)
        return (grad_k, grad_v)

    grad_k, grad_v = lax.fori_loop(0, piece_count // sub_rows, sub_step, fold_start)
    grad_queries = rotate(grad_q, cos_table, sin_table, -1.0).astype(jnp.bfloat16)[:, None, :]
    grad_keys = rotate(grad_k, cos_table, sin_table, -1.0).astype(jnp.bfloat16)[:, None, :]
    grad_values = grad_v.astype(jnp.bfloat16)[:, None, :]
    return (grad_queries, grad_keys, grad_values)


def solution(mesh):
    in_specs = (
        P(("dp", "seq"), "tm", None),
        P(("dp", "seq"), "tm", None),
        P(("dp", "seq"), "tm", None),
        P("seq"),
        P("tm", None, None),
        P(),
        P(),
        P("dp"),
        P(("dp", "tm"), "seq", None),
    )
    out_specs = (
        P(("dp", "seq"), "tm", None),
        P(("dp", "seq"), "tm", None),
        P(("dp", "seq"), "tm", None),
    )
    return jax.shard_map(
        on_device, mesh=mesh, in_specs=in_specs, out_specs=out_specs, check_vma=False
    )
```

profile of v0, /device:TPU:4, one launch (start us, length us, event | category | flops | bytes accessed | tf_op | source)
XLA Modules:
  0.0 426.8 jit_solution(6514035259708986628)
XLA Ops:
  13.6 73.2 %all-gather.8.cloned.1.call-done = bf16[8192,128]{0,1:T(8,128)(2,1)} async-done(((bf16[512,128]{0,1:T(8,128)(2,1)}), bf16[8192,128]{0,1:T(8,128)(2,1)}) %all-gather.8.cloned.1.call-update) | async-done | bytes 2097168 | tf_op jit(solution)/shard_map/all_gather | solution.py:91
  86.8 4.1 copy.61
  90.9 66.2 %all-gather.14.cloned.1.call-done = bf16[8192,1,128]{2,0,1:T(8,128)(2,1)} async-done(((bf16[512,1,128]{2,0,1:T(8,128)(2,1)}), bf16[8192,1,128]{2,0,1:T(8,128)(2,1)}) %all-gather.14.cloned.1.call-update) | async-done | bytes 2097168 | tf_op jit(solution)/shard_map/all_gather | solution.py:92
  157.2 26.8 %while.48 = (s32[]{:T(128)}, f32[512]{0:T(512)S(1)}, f32[512]{0:T(512)S(1)}, f32[512,128]{1,0:T(8,128)S(1)}, bf16[8192,128]{1,0:T(8,128)(2,1)}, /*index=5*/bf16[...) while((s32[]{:T(128)}, f32[512]{0:T(512)S(1)}, ...), condition=%wide.region_3.4_spmd.clone, body=%wide.region_0.3_spmd.clone.sunk | while | flops 272828928 | bytes 7504047 | solution.py:117
  157.2 1.4 multiply_reduce_fusion.5
  159.0 1.5 convolution_add_fusion.4
  160.5 1.4 multiply_reduce_fusion.5
  162.3 1.5 convolution_add_fusion.4
  165.7 1.5 convolution_add_fusion.4
  169.0 1.5 convolution_add_fusion.4
  170.6 1.4 multiply_reduce_fusion.5
  172.4 1.5 convolution_add_fusion.4
  175.7 1.5 convolution_add_fusion.4
  179.1 1.5 convolution_add_fusion.4
  180.6 1.4 multiply_reduce_fusion.5
  182.4 1.5 convolution_add_fusion.4
  185.9 1.9 collective-permute-start
  190.8 34.3 %all-gather.1 = f32[16,1,512]{2,1,0:T(1,128)} all-gather(f32[1,1,512]{2,1,0:T(1,128)S(1)} %bitcast.108), channel_id=1, replica_groups=mesh['seq'=16,'tm'=8,'dp'=2] {'seq'}, dimensions={0}, use_global_device_ids=true | all-gather | bytes 34816 | tf_op jit(solution)/shard_map/all_gather | solution.py:181
  228.3 11.8 %all_gather.23 = bf16[512,384]{1,0:T(8,128)(2,1)S(1)} all-gather(bf16[64,384]{1,0:T(8,128)(2,1)S(1)} %bitcast.103), channel_id=1, replica_groups=mesh['seq'=16,'tm'=8,'dp'=2] {'tm'}, dimensions={0}, use_global_device_ids=true | all-gather | bytes 442368 | tf_op jit(solution)/shard_map/all_gather | solution.py:157
  241.6 35.1 %while.49 = (s32[]{:T(128)}, f32[512,128]{1,0:T(8,128)}, bf16[8192,128]{1,0:T(8,128)(2,1)}, bf16[512,128]{1,0:T(8,128)(2,1)S(1)}, f32[512]{0:T(512)}, /*index=5*...) while((s32[]{:T(128)}, f32[512,128]{1,0:T(8,128)}, ...), condition=%wide.region_9.10_spmd.clone, body=%wide.region_8.9_spmd.clone.sunk | while | flops 405471232 | bytes 7886624 | solution.py:175
  241.7 1.4 fusion.121
  243.1 2.2 fusion.122
  246.0 1.4 fusion.121
  247.5 2.2 fusion.122
  250.4 1.4 fusion.121
  251.9 2.2 fusion.122
  254.8 1.4 fusion.121
  256.3 2.2 fusion.122
  259.2 1.4 fusion.121
  260.7 2.2 fusion.122
  263.6 1.4 fusion.121
  265.0 2.2 fusion.122
  267.9 1.4 fusion.121
  269.4 2.2 fusion.122
  272.3 1.4 fusion.121
  273.8 2.2 fusion.122
  278.0 32.2 %all-gather.2 = f32[16,1,512]{2,1,0:T(1,128)} all-gather(f32[1,1,512]{2,1,0:T(1,128)} %bitcast.109), channel_id=1, replica_groups=mesh['seq'=16,'tm'=8,'dp'=2] {'seq'}, dimensions={0}, use_global_device_ids=true | all-gather | bytes 34816 | tf_op jit(solution)/shard_map/all_gather | solution.py:182
  311.0 48.9 %all-gather.12.cloned.1.call-done = bf16[8192,128]{0,1:T(8,128)(2,1)} async-done(((bf16[512,128]{0,1:T(8,128)(2,1)}), bf16[8192,128]{0,1:T(8,128)(2,1)}) %all-gather.12.cloned.1.call-update) | async-done | bytes 2097168 | tf_op jit(solution)/shard_map/all_gather | solution.py:180
  359.9 54.8 %while.50 = (s32[]{:T(128)}, f32[512,128]{1,0:T(8,128)}, f32[512,128]{1,0:T(8,128)S(1)}, bf16[8192,128]{0,1:T(8,128)(2,1)}, bf16[512,128]{1,0:T(8,128)(2,1)S(1)}...) while((s32[]{:T(128)}, f32[512,128]{1,0:T(8,128)}, ...), condition=%wide.region_11.12_spmd.clone, body=%wide.region_10.11_spmd.clone.sunk | while | flops 541392896 | bytes 11301086 | solution.py:201
  364.0 2.0 fusion.131
  370.0 2.9 fusion.131
  376.9 2.9 fusion.131
  383.9 2.9 fusion.131
  390.9 2.9 fusion.131
  397.8 2.9 fusion.131
  404.8 2.9 fusion.131
  411.8 2.9 fusion.131
  416.1 1.5 subtract_convert_fusion
  (282 shorter events, 68.7 us)
Async XLA Ops:
  7.2 177.0 %copy-start = (bf16[1,128,384]{2,1,0:T(8,128)(2,1)S(1)}, bf16[1,128,384]{2,1,0:T(8,128)(2,1)}, u32[]{:S(2)}) copy-start(bf16[1,128,384]{2,1,0:T(8,128)(2,1)} %param.19) | copy-start | bytes 294916
  7.2 79.6 %all-gather.8.cloned.1.call-start = ((), (), s32[]{:S(2)}) async-start(), calls=%async_computation.1 | async-start | bytes 2228224 | tf_op jit(solution)/shard_map/all_gather | solution.py:91
  10.9 80.0 %copy-start.6 = (f32[512,21,1]{0,1,2:T(8,128)}, f32[512,21,1]{0,1,2:T(8,128)S(1)}, u32[]{:S(2)}) copy-start(f32[512,21,1]{0,1,2:T(8,128)S(1)} %get-tuple-element.690) | copy-start | bytes 129028
  10.9 80.0 %copy-start.7 = (f32[512,21,1]{0,1,2:T(8,128)}, f32[512,21,1]{0,1,2:T(8,128)S(1)}, u32[]{:S(2)}) copy-start(f32[512,21,1]{0,1,2:T(8,128)S(1)} %get-tuple-element.691) | copy-start | bytes 129028
  12.4 144.7 %all-gather.14.cloned.1.call-start = ((), (), s32[]{:S(2)}) async-start(), calls=%async_computation.5 | async-start | bytes 2228224 | tf_op jit(solution)/shard_map/all_gather | solution.py:92
  13.2 212.0 %reduce-scatter.2.cloned.1.call-start = ((), (), s32[]{:S(2)}) async-start(), calls=%async_computation.2 | async-start | bytes 442368 | tf_op jit(solution)/shard_map/reduce_scatter | solution.py:122
  13.4 77.5 %copy-start.2 = (bf16[512,128]{0,1:T(8,128)(2,1)}, bf16[512,128]{0,1:T(8,128)(2,1)S(1)}, u32[]{:S(2)}) copy-start(bf16[512,128]{0,1:T(8,128)(2,1)S(1)} %convert_element_type.145) | copy-start | bytes 393220
  184.0 6.8 %copy-start.12 = (f32[512]{0:T(512)}, f32[512]{0:T(512)S(1)}, u32[]{:S(2)}) copy-start(f32[512]{0:T(512)S(1)} %get-tuple-element.424) | copy-start | bytes 6148
  184.0 1.9 copy-start.11
  184.0 3.9 copy-start.1
  184.0 6.0 %copy-start.4 = (bf16[3,384,768]{2,1,0:T(8,128)(2,1)S(1)}, bf16[3,384,768]{2,1,0:T(8,128)(2,1)}, u32[]{:S(2)}) copy-start(bf16[3,384,768]{2,1,0:T(8,128)(2,1)} %param.21) | copy-start | bytes 5308420
  184.1 6.2 %copy-start.3 = (bf16[512,128]{0,1:T(8,128)(2,1)S(1)}, bf16[512,128]{0,1:T(8,128)(2,1)}, u32[]{:S(2)}) copy-start(bf16[512,128]{0,1:T(8,128)(2,1)} %convert_element_type.142) | copy-start | bytes 393220
  185.2 41.8 %copy-start.17 = (f32[384]{0:T(512)S(1)}, f32[384]{0:T(512)}, u32[]{:S(2)}) copy-start(f32[384]{0:T(512)} %param.20) | copy-start | bytes 4612
  185.3 125.7 %all-gather.10.cloned.1.call-start = ((), (), s32[]{:S(2)}) async-start(), calls=%async_computation.3 | async-start | bytes 2228224 | tf_op jit(solution)/shard_map/all_gather | solution.py:179
  185.8 174.1 %all-gather.12.cloned.1.call-start = ((), (), s32[]{:S(2)}) async-start(), calls=%async_computation.4 | async-start | bytes 2228224 | tf_op jit(solution)/shard_map/all_gather | solution.py:180
  185.9 4.6 %collective-permute-start = (bf16[2,32,768]{2,1,0:T(8,128)(2,1)S(1)}, bf16[2,32,768]{2,1,0:T(8,128)(2,1)S(1)}, u32[]{:S(2)}, u32[]{:S(2)}) collective-permute-start(bf16[2,32,768]{2,1,0:T(8,128)(2,1)S(1)} %copy-done.11), channel_id=1, source_target_pairs={{2,0},{4,2},{6,4},{8,6},{10,8},{12,10},{14,12},{3,1},{5,3},{7,5},{... | collective-permute-start | bytes 294920 | tf_op jit(solution)/shard_map/ppermute | solution.py:14
  190.8 36.2 %copy-start.14 = (f32[512]{0:T(512)}, f32[512]{0:T(512)S(1)}, u32[]{:S(2)}) copy-start(f32[512]{0:T(512)S(1)} %log_add_fusion) | copy-start | bytes 6148
  190.8 49.3 %copy-start.13 = (f32[512]{0:T(512)S(1)}, f32[512]{0:T(512)}, u32[]{:S(2)}) copy-start(f32[512]{0:T(512)} %copy-done.12) | copy-start | bytes 6148
  241.6 1.5 copy-start.8
  241.6 1.5 copy-start.15
  241.6 1.5 copy-start.16
  246.0 1.4 copy-start.8
  246.0 1.4 copy-start.15
  246.0 1.5 copy-start.16
  250.4 1.4 copy-start.15
  250.4 1.5 copy-start.16
  254.8 1.4 copy-start.8
  254.8 1.5 copy-start.15
  254.8 1.5 copy-start.16
  259.2 1.4 copy-start.8
  259.2 1.4 copy-start.15
  259.2 1.5 copy-start.16
  263.6 1.4 copy-start.8
  263.6 1.4 copy-start.15
  263.6 1.5 copy-start.16
  267.9 1.4 copy-start.15
  267.9 1.5 copy-start.16
  272.3 1.4 copy-start.8
  272.3 1.5 copy-start.15
  272.3 1.5 copy-start.16
  361.8 2.2 copy-start.10
  367.8 2.2 copy-start.10
  374.7 2.2 copy-start.10
  381.7 2.2 copy-start.10
  388.7 2.2 copy-start.10
  395.6 2.2 copy-start.10
  402.6 2.2 copy-start.10
  409.6 2.2 copy-start.10
  (11 other events, 9.3 us)
Sparse Core Ops, SparseCore 0:
  12.5 74.2 all-gather.7
  88.6 68.5 all-gather.13
  185.4 26.1 reduce-scatter.1
  213.8 75.1 all-gather.9
  291.2 68.6 all-gather.11
where the time goes:
time: 429 us; the launch traced here: 427 us
  waiting for transfers between devices  190 us (44%)
  matrix products  86.8 us (20%)
  blocking collectives  78.3 us (18%)
  local copies, waits for them, and re-layouts  45.6 us (11%)
  between operations  14.3 us (3%)
  other arithmetic  9.06 us (2%)
    all_gather x1, waiting for transfers between devices, on_device(): lax.all_gather(rot_k, 'seq', axis=0, tiled=True)  73.2 us
    all_gather x1, waiting for transfers between devices, on_device(): lax.all_gather(plain_v, 'seq', axis=0, tiled=True)  66.2 us
    all_gather x1, waiting for transfers between devices, on_device(): piece_grad = lax.all_gather(wide_grad, 'seq', axis=0, tiled=True)  48.9 us
    all_gather x1, blocking collectives, on_device(): piece_log = lax.all_gather(log_total, 'seq', axis=0, tiled=True)  34.3 us
    all_gather x1, blocking collectives, on_device(): piece_delta = lax.all_gather(row_delta, 'seq', axis=0, tiled=True)  32.2 us
    dot_general x16, matrix products, inner(): lax.dot_general(left, right, (((0,), (0,)), ((), ())), preferred_element_...  28.5 us
    dot_general x25, matrix products, cross(): lax.dot_general(left, right, (((1,), (1,)), ((), ())), preferred_element_...  26.9 us
    dot_general x8, matrix products, query_step(): jnp.dot(grad_s, key_piece, preferred_element_type=jnp.float32) * score_scale  17.4 us
  transfers between devices with their start and end apart: 6, of which 3 were waited for; matrix products, arithmetic and copies ran while one was open for 10% of the time, Pallas kernels for 0%

commit v1 on v0

--- a/solution.py
+++ b/solution.py
@@ -87,9 +87,22 @@
         jnp.bfloat16
     )
     plain_v = values[:, 0, :]
+
+    def expand_blocks(block_here, mesh_ax):
+        y_new = jnp.concatenate(
+            jax.lax.all_to_all(
+                jnp.stack(tuple((block_here for _ in range(jax.lax.axis_size(mesh_ax)))), 0),
+                axis_name=mesh_ax,
+                split_axis=0,
+                concat_axis=0,
+            ),
+            0,
+        )
+        return y_new
+
     keys_all, values_all = (
         lax.all_gather(rot_k, "seq", axis=0, tiled=True),
-        lax.all_gather(plain_v, "seq", axis=0, tiled=True),
+        expand_blocks(plain_v, "seq"),
     )
     total_tokens = keys_all.shape[0]
     key_block = math.gcd(total_tokens, 1024)

time: 429 us -> 386 us (0.90)
  waiting for transfers between devices: 190 us -> 142 us
  starting transfers between devices: 2.12 us -> 11.7 us
  local copies, waits for them, and re-layouts: 45.6 us -> 40.6 us
    all_gather x1 -> x0, waiting for transfers between devices: 66.2 us -> none  [on_device(): lax.all_gather(plain_v, 'seq', axis=0, tiled=True)]
    all_gather x1, waiting for transfers between devices: 73.2 us -> 84.1 us  [on_device(): lax.all_gather(rot_k, 'seq', axis=0, tiled=True)]
    all_to_all x0 -> x1, starting transfers between devices: none -> 9.63 us  [expand_blocks(): jax.lax.all_to_all(jnp.stack(tuple((block_here for _ in range(jax.lax.axi...]
    all_gather x1, waiting for transfers between devices: 48.9 us -> 57.1 us  [on_device(): piece_grad = lax.all_gather(wide_grad, 'seq', axis=0, tiled=True)]
    while x88 -> x24, local copies, waits for them, and re-layouts: 5.89 us -> 0.07 us
  transfers between devices with their start and end apart: 6 -> 6, of which waited for: 3 -> 2; matrix products, arithmetic and copies ran while one was open for 10% -> 11% of each run, Pallas kernels for 0% -> 0%
where the time goes in v1:
time: 386 us; the launch traced here: 384 us
  waiting for transfers between devices  142 us (37%)
  matrix products  86 us (22%)
  blocking collectives  79.1 us (20%)
  local copies, waits for them, and re-layouts  40.6 us (11%)
  between operations  14.3 us (4%)
  starting transfers between devices  11.7 us (3%)
  other arithmetic  9.06 us (2%)
    all_gather x1, waiting for transfers between devices, on_device(): lax.all_gather(rot_k, 'seq', axis=0, tiled=True)  84.1 us
    all_gather x1, waiting for transfers between devices, on_device(): piece_grad = lax.all_gather(wide_grad, 'seq', axis=0, tiled=True)  57.1 us
    all_gather x1, blocking collectives, on_device(): piece_log = lax.all_gather(log_total, 'seq', axis=0, tiled=True)  35.1 us
    all_gather x1, blocking collectives, on_device(): piece_delta = lax.all_gather(row_delta, 'seq', axis=0, tiled=True)  32.2 us
    dot_general x16, matrix products, inner(): lax.dot_general(left, right, (((0,), (0,)), ((), ())), preferred_element_...  28.7 us
    dot_general x25, matrix products, cross(): lax.dot_general(left, right, (((1,), (1,)), ((), ())), preferred_element_...  26 us
    dot_general x8, matrix products, query_step(): jnp.dot(grad_s, key_piece, preferred_element_type=jnp.float32) * score_scale  17.4 us
    dot_general x8, matrix products, forward_step(): jnp.dot(weights.astype(jnp.bfloat16), value_piece, preferred_element_type...  11.9 us
  transfers between devices with their start and end apart: 6, of which 2 were waited for; matrix products, arithmetic and copies ran while one was open for 11% of the time, Pallas kernels for 0%

profile of v1, /device:TPU:4, one launch (start us, length us, event | category | flops | bytes accessed | tf_op | source)
XLA Modules:
  0.0 383.6 jit_solution(14783803015154764872)
XLA Ops:
  12.5 1.7 stack.47
  14.2 9.6 %all-to-all-start = ((bf16[16,512,128]{2,1,0:T(8,128)(2,1)}), bf16[16,512,128]{2,1,0:T(8,128)(2,1)}, u32[]{:S(2)}, u32[]{:S(2)}) async-start(bf16[16,512,128]{2,1,0:T(8,128)(2,1)} %stack.47), calls=%async_computation | async-start | bytes 4194304 | tf_op jit(solution)/shard_map/all_to_all | solution.py:93
  24.2 84.1 %all-gather.6.cloned.1.call-done = bf16[8192,128]{0,1:T(8,128)(2,1)} async-done(((bf16[512,128]{0,1:T(8,128)(2,1)}), bf16[8192,128]{0,1:T(8,128)(2,1)}) %all-gather.6.cloned.1.call-update) | async-done | bytes 2097168 | tf_op jit(solution)/shard_map/all_gather | solution.py:104
  108.4 4.1 %copy.61 = bf16[8192,128]{1,0:T(8,128)(2,1)} copy(bf16[8192,128]{0,1:T(8,128)(2,1)} %all-gather.6.cloned.1.call-done) | data formatting | bytes 4194304
  112.5 26.8 %while.48 = (s32[]{:T(128)}, f32[512]{0:T(512)S(1)}, f32[512]{0:T(512)S(1)}, f32[512,128]{1,0:T(8,128)S(1)}, bf16[8192,128]{1,0:T(8,128)(2,1)}, /*index=5*/bf16[...) while((s32[]{:T(128)}, f32[512]{0:T(512)S(1)}, ...), condition=%wide.region_3.4_spmd.clone, body=%wide.region_0.3_spmd.clone.sunk | while | flops 272828928 | bytes 7504047 | solution.py:130
  112.5 1.4 multiply_reduce_fusion.5
  114.4 1.5 convolution_add_fusion.4
  115.9 1.4 multiply_reduce_fusion.5
  117.7 1.5 convolution_add_fusion.4
  119.2 1.4 multiply_reduce_fusion.5
  121.1 1.5 convolution_add_fusion.4
  122.6 1.4 multiply_reduce_fusion.5
  124.4 1.5 convolution_add_fusion.4
  125.9 1.4 multiply_reduce_fusion.5
  127.8 1.5 convolution_add_fusion.4
  129.3 1.4 multiply_reduce_fusion.5
  131.1 1.5 convolution_add_fusion.4
  132.6 1.4 multiply_reduce_fusion.5
  134.5 1.5 convolution_add_fusion.4
  136.0 1.4 multiply_reduce_fusion.5
  137.8 1.5 convolution_add_fusion.4
  141.4 1.9 collective-permute-start
  146.3 35.1 %all-gather = f32[16,1,512]{2,1,0:T(1,128)} all-gather(f32[1,1,512]{2,1,0:T(1,128)S(1)} %bitcast.108), channel_id=1, replica_groups=mesh['seq'=16,'tm'=8,'dp'=2] {'seq'}, dimensions={0}, use_global_device_ids=true | all-gather | bytes 34816 | tf_op jit(solution)/shard_map/all_gather | solution.py:194
  184.6 11.8 %all_gather.19 = bf16[512,384]{1,0:T(8,128)(2,1)S(1)} all-gather(bf16[64,384]{1,0:T(8,128)(2,1)S(1)} %bitcast.102), channel_id=1, replica_groups=mesh['seq'=16,'tm'=8,'dp'=2] {'tm'}, dimensions={0}, use_global_device_ids=true | all-gather | bytes 442368 | tf_op jit(solution)/shard_map/all_gather | solution.py:170
  197.3 28.8 %while.49 = (s32[]{:T(128)}, f32[512,128]{1,0:T(8,128)S(1)}, bf16[8192,128]{1,0:T(8,128)(2,1)}, bf16[512,128]{1,0:T(8,128)(2,1)S(1)}, f32[512]{0:T(512)S(1)}, /*...) while((s32[]{:T(128)}, f32[512,128]{1,0:T(8,128)S(1)}, ...), condition=%wide.region_9.10_spmd.clone, body=%wide.region_8.9_spmd.clone.sunk | while | flops 405471232 | bytes 5772976 | solution.py:188
  198.7 2.2 fusion.122
  200.9 1.4 fusion.121
  202.3 2.2 fusion.122
  204.5 1.4 fusion.121
  205.9 2.2 fusion.122
  209.5 2.2 fusion.122
  211.7 1.4 fusion.121
  213.1 2.2 fusion.122
  216.7 2.2 fusion.122
  220.3 2.2 fusion.122
  223.9 2.2 fusion.122
  226.4 32.2 %all-gather.1 = f32[16,1,512]{2,1,0:T(1,128)} all-gather(f32[1,1,512]{2,1,0:T(1,128)S(1)} %bitcast.109), channel_id=1, replica_groups=mesh['seq'=16,'tm'=8,'dp'=2] {'seq'}, dimensions={0}, use_global_device_ids=true | all-gather | bytes 34816 | tf_op jit(solution)/shard_map/all_gather | solution.py:195
  259.4 57.1 %all-gather.10.cloned.1.call-done = bf16[8192,128]{0,1:T(8,128)(2,1)} async-done(((bf16[512,128]{0,1:T(8,128)(2,1)}), bf16[8192,128]{0,1:T(8,128)(2,1)}) %all-gather.10.cloned.1.call-update) | async-done | bytes 2097168 | tf_op jit(solution)/shard_map/all_gather | solution.py:193
  316.5 55.0 %while.50 = (s32[]{:T(128)}, f32[512,128]{1,0:T(8,128)}, f32[512,128]{1,0:T(8,128)S(1)}, bf16[8192,128]{0,1:T(8,128)(2,1)}, bf16[512,128]{1,0:T(8,128)(2,1)S(1)}...) while((s32[]{:T(128)}, f32[512,128]{1,0:T(8,128)}, ...), condition=%wide.region_11.12_spmd.clone, body=%wide.region_10.11_spmd.clone.sunk | while | flops 541392896 | bytes 11301086 | solution.py:214
  320.6 2.0 fusion.131
  326.6 2.9 fusion.131
  333.6 2.9 fusion.131
  340.6 2.9 fusion.131
  347.6 2.9 fusion.131
  354.6 2.9 fusion.131
  361.5 2.9 fusion.131
  368.5 2.9 fusion.131
  372.9 1.5 subtract_convert_fusion
  (214 shorter events, 62.2 us)
Async XLA Ops:
  7.2 132.3 %copy-start = (bf16[1,128,384]{2,1,0:T(8,128)(2,1)S(1)}, bf16[1,128,384]{2,1,0:T(8,128)(2,1)}, u32[]{:S(2)}) copy-start(bf16[1,128,384]{2,1,0:T(8,128)(2,1)} %param.19) | copy-start | bytes 294916
  7.2 101.2 %all-gather.6.cloned.1.call-start = ((), (), s32[]{:S(2)}) async-start(), calls=%async_computation.2 | async-start | bytes 2228224 | tf_op jit(solution)/shard_map/all_gather | solution.py:104
  9.2 3.3 copy-start.8
  10.9 0.6 copy-start.6
  11.0 0.6 copy-start.7
  14.2 98.3 %all-to-all-start = ((bf16[16,512,128]{2,1,0:T(8,128)(2,1)}), bf16[16,512,128]{2,1,0:T(8,128)(2,1)}, u32[]{:S(2)}, u32[]{:S(2)}) async-start(bf16[16,512,128]{2,1,0:T(8,128)(2,1)} %stack.47), calls=%async_computation | async-start | bytes 4194304 | tf_op jit(solution)/shard_map/all_to_all | solution.py:93
  23.8 157.6 %reduce-scatter.2.cloned.1.call-start = ((), (), s32[]{:S(2)}) async-start(), calls=%async_computation.3 | async-start | bytes 442368 | tf_op jit(solution)/shard_map/reduce_scatter | solution.py:135
  24.1 88.4 %copy-start.2 = (bf16[512,128]{0,1:T(8,128)(2,1)}, bf16[512,128]{0,1:T(8,128)(2,1)S(1)}, u32[]{:S(2)}) copy-start(bf16[512,128]{0,1:T(8,128)(2,1)S(1)} %convert_element_type.145) | copy-start | bytes 393220
  139.3 2.0 copy-start.10
  139.3 4.0 %copy-start.1 = (s32[16]{0:T(128)S(1)}, s32[16]{0:T(128)}, u32[]{:S(2)}) copy-start(s32[16]{0:T(128)} %param.22) | copy-start | bytes 196
  139.4 6.1 %copy-start.4 = (bf16[3,384,768]{2,1,0:T(8,128)(2,1)S(1)}, bf16[3,384,768]{2,1,0:T(8,128)(2,1)}, u32[]{:S(2)}) copy-start(bf16[3,384,768]{2,1,0:T(8,128)(2,1)} %param.21) | copy-start | bytes 5308420
  139.5 6.3 %copy-start.3 = (bf16[512,128]{0,1:T(8,128)(2,1)S(1)}, bf16[512,128]{0,1:T(8,128)(2,1)}, u32[]{:S(2)}) copy-start(bf16[512,128]{0,1:T(8,128)(2,1)} %convert_element_type.142) | copy-start | bytes 393220
  140.6 42.7 %copy-start.11 = (f32[384]{0:T(512)S(1)}, f32[384]{0:T(512)}, u32[]{:S(2)}) copy-start(f32[384]{0:T(512)} %param.20) | copy-start | bytes 4612
  140.6 118.9 %all-gather.8.cloned.1.call-start = ((), (), s32[]{:S(2)}) async-start(), calls=%async_computation.4 | async-start | bytes 2228224 | tf_op jit(solution)/shard_map/all_gather | solution.py:192
  141.3 175.2 %all-gather.10.cloned.1.call-start = ((), (), s32[]{:S(2)}) async-start(), calls=%async_computation.5 | async-start | bytes 2228224 | tf_op jit(solution)/shard_map/all_gather | solution.py:193
  141.4 4.6 %collective-permute-start = (bf16[2,32,768]{2,1,0:T(8,128)(2,1)S(1)}, bf16[2,32,768]{2,1,0:T(8,128)(2,1)S(1)}, u32[]{:S(2)}, u32[]{:S(2)}) collective-permute-start(bf16[2,32,768]{2,1,0:T(8,128)(2,1)S(1)} %copy-done.10), channel_id=1, source_target_pairs={{2,0},{4,2},{6,4},{8,6},{10,8},{12,10},{14,12},{3,1},{5,3},{7,5},{... | collective-permute-start | bytes 294920 | tf_op jit(solution)/shard_map/ppermute | solution.py:14
  196.6 0.7 copy-start.5
  318.3 2.2 copy-start.9
  324.4 2.2 copy-start.9
  331.4 2.2 copy-start.9
  338.4 2.2 copy-start.9
  345.3 2.2 copy-start.9
  352.3 2.2 copy-start.9
  359.3 2.2 copy-start.9
  366.3 2.2 copy-start.9
Sparse Core Ops, SparseCore 0:
  12.6 95.7 all-gather.5
  140.7 27.0 reduce-scatter.1
  170.2 75.2 all-gather.7
  247.7 68.6 all-gather.9
